TPU v7x, 32 devices: a whole 2x2x4 slice. The times are simulated.
32 devices in a mesh: dp: 4 (over z), fsdp: 2 (over x), rows: 4 (over y, core).
Axes of the slice: x: 2, y: 2, z: 4, core: 2. Of those that a mesh axis runs over, the one named last changes fastest.
Arguments:
- feature_maps: bfloat16 [8, 16, 32, 1536], P(('dp', 'fsdp'), 'rows'), may hold values from -30 to 30
- dw_kernel: float32 [7, 7, 1536], replicated, may hold values from -0.875 to 0.875
- norm_gain: float32 [1536], replicated, may hold values from 0.5 to 1.5
- w_up: bfloat16 [1536, 6144], P(('dp', 'rows'), 'fsdp'), may hold values from -0.15625 to 0.15625
- w_down: bfloat16 [6144, 1536], P('fsdp', ('dp', 'rows')), may hold values from -0.078125 to 0.078125
- layer_scale: float32 [1536], replicated, may hold values from 0.3 to 1.5
- d_out: bfloat16 [8, 16, 32, 1536], P(('dp', 'fsdp'), 'rows'), may hold values from -20 to 20
Outputs:
- result: bfloat16 [8, 16, 32, 1536], P(('dp', 'fsdp'), 'rows')
- grad_x: bfloat16 [8, 16, 32, 1536], P(('dp', 'fsdp'), 'rows')
- grad_up: float32 [1536, 6144], P(('dp', 'rows'), 'fsdp')
- grad_down: float32 [6144, 1536], P('fsdp', ('dp', 'rows'))
- grad_kernel: float32 [7, 7, 1536], replicated
- grad_gain: float32 [1536], replicated
- grad_scale: float32 [1536], replicated
All inputs are finite; a program needn't handle non-finite values.
Results may differ from a plain program's by a relative error of at most 0.0075.
Values may be sent and summed in bfloat16 or wider, within the bound.
No kernel may reach another device: no remote copies, remote signals or barrier semaphores. Data moves between devices by JAX's collectives and lax.ppermute only.
A program may use at most 128 MiB of HBM per device.

v0:
```python
import math
import jax
import jax.numpy as jnp
from jax import lax
from jax.sharding import PartitionSpec as P

KS = 7
norm_eps = 1e-06
inv_root_two = 1.0 / math.sqrt(2.0)
inv_root_two_pi = 1.0 / math.sqrt(2.0 * math.pi)
contract_rows = (((0,), (0,)), ((), ()))
contract_cols = (((1,), (1,)), ((), ()))


def padded_2(x, sides, width):
    for axis, dim in sides:
        devices, length = (lax.axis_size(axis), x.shape[dim])
        up = [(i, (i + 1) % devices) for i in range(devices - 1)]
        down = [(j, i) for i, j in up]
        last = lax.slice_in_dim(x, length - width, length, axis=dim)
        leading = lax.slice_in_dim(x, 0, width, axis=dim)
        before = lax.ppermute(last, axis, up)
        after = lax.ppermute(leading, axis, down)
        x = jnp.concatenate([before, x, after], axis=dim)
    return x


def gelu_exact(values):
    return 0.5 * values * (1.0 + jax.scipy.special.erf(values * inv_root_two))


def gelu_slope(values):
    cdf_part = 0.5 * (1.0 + jax.scipy.special.erf(values * inv_root_two))
    return cdf_part + values * jnp.exp(-0.5 * values * values) * inv_root_two_pi


def reduce_down(down_part):
    return lax.psum_scatter(down_part, ("dp", "rows"), scatter_dimension=1, tiled=True)


def body(feature_maps, dw_kernel, norm_gain, w_up, w_down, layer_scale, d_out):
    scenes, strip, across, width = feature_maps.shape
    cells = scenes * strip * across
    rimmed = padded_2(feature_maps, (("rows", 1),), 3)
    padded = jnp.pad(rimmed.astype(jnp.float32), ((0, 0), (0, 0), (3, 3), (0, 0)))
    filtered = jnp.zeros(feature_maps.shape, jnp.float32)
    for row_off in range(KS):
        for col_off in range(KS):
            filtered = (
                filtered
                + padded[:, row_off : row_off + strip, col_off : col_off + across, :]
                * dw_kernel[row_off, col_off]
            )
    flat = filtered.reshape(cells, width)
    average = jnp.mean(flat, axis=-1, keepdims=True)
    center = flat - average
    variance = jnp.mean(center * center, axis=-1, keepdims=True)
    rstd = lax.rsqrt(variance + norm_eps)
    normed = center * rstd
    scaled = (normed * norm_gain).astype(jnp.bfloat16)
    gathered = lax.all_gather(scaled, "fsdp", axis=0, tiled=True)
    up_full = lax.all_gather(w_up, ("dp", "rows"), axis=0, tiled=True)
    down_full = lax.all_gather(w_down, ("dp", "rows"), axis=1, tiled=True)
    hidden = jnp.dot(gathered, up_full, preferred_element_type=jnp.float32)
    active = gelu_exact(hidden).astype(jnp.bfloat16)
    mlp_terms = jnp.dot(active, down_full, preferred_element_type=jnp.float32)
    branch = lax.psum_scatter(
        mlp_terms.astype(jnp.bfloat16), "fsdp", scatter_dimension=0, tiled=True
    ).astype(jnp.float32)
    resid = feature_maps.reshape(cells, width).astype(jnp.float32)
    result = (resid + layer_scale * branch).astype(jnp.bfloat16).reshape(feature_maps.shape)
    cotan = d_out.reshape(cells, width).astype(jnp.float32)
    scale_part = jnp.sum(cotan * branch, axis=0)
    back = (cotan * layer_scale).astype(jnp.bfloat16)
    back_all = lax.all_gather(back, "fsdp", axis=0, tiled=True)
    down_part = lax.dot_general(active, back_all, contract_rows, preferred_element_type=jnp.float32)
    slope_in = lax.dot_general(
        back_all, down_full, contract_cols, preferred_element_type=jnp.float32
    )
    hidden_grad = (slope_in * gelu_slope(hidden)).astype(jnp.bfloat16)
    up_part = lax.dot_general(
        gathered, hidden_grad, contract_rows, preferred_element_type=jnp.float32
    )
    norm_terms = lax.dot_general(
        hidden_grad, up_full, contract_cols, preferred_element_type=jnp.float32
    )
    norm_grad = lax.psum_scatter(norm_terms, "fsdp", scatter_dimension=0, tiled=True)
    grad_up = lax.psum_scatter(up_part, ("dp", "rows"), scatter_dimension=0, tiled=True)
    grad_down = reduce_down(down_part)
    gain_part = jnp.sum(norm_grad * normed, axis=0)
    scaled_grad = norm_grad * norm_gain
    conv_grad = rstd * (
        scaled_grad
        - jnp.mean(scaled_grad, axis=-1, keepdims=True)
        - normed * jnp.mean(scaled_grad * normed, axis=-1, keepdims=True)
    )
    conv_grad = conv_grad.reshape(feature_maps.shape)
    grad_rim = padded_2(conv_grad.astype(jnp.bfloat16), (("rows", 1),), 3).astype(conv_grad.dtype)
    grad_pad = jnp.pad(grad_rim, ((0, 0), (0, 0), (3, 3), (0, 0)))
    kernel_rows = []
    back_conv = jnp.zeros(feature_maps.shape, jnp.float32)
    for row_off in range(KS):
        for col_off in range(KS):
            window = padded[:, row_off : row_off + strip, col_off : col_off + across, :]
            kernel_rows.append(jnp.sum(window * conv_grad, axis=(0, 1, 2)))
            back_conv = (
                back_conv
                + grad_pad[
                    :, 6 - row_off : 6 - row_off + strip, 6 - col_off : 6 - col_off + across, :
                ]
                * dw_kernel[row_off, col_off]
            )
    kernel_part = jnp.stack(kernel_rows).reshape(KS, KS, width)
    grad_x = (d_out.astype(jnp.float32) + back_conv).astype(jnp.bfloat16)
    grad_kernel, grad_gain, grad_scale = lax.psum(
        (kernel_part, gain_part, scale_part), ("dp", "fsdp", "rows")
    )
    return (result, grad_x, grad_up, grad_down, grad_kernel, grad_gain, grad_scale)


def solution(mesh):
    return jax.shard_map(
        body,
        mesh=mesh,
        in_specs=(
            P(("dp", "fsdp"), "rows", None, None),
            P(),
            P(),
            P(("dp", "rows"), "fsdp"),
            P("fsdp", ("dp", "rows")),
            P(),
            P(("dp", "fsdp"), "rows", None, None),
        ),
        out_specs=(
            P(("dp", "fsdp"), "rows", None, None),
            P(("dp", "fsdp"), "rows", None, None),
            P(("dp", "rows"), "fsdp"),
            P("fsdp", ("dp", "rows")),
            P(),
            P(),
            P(),
        ),
        check_vma=False,
    )
```

profile of v0, /device:TPU:0, one launch (start us, length us, event | category | flops | bytes accessed | tf_op | source)
XLA Modules:
  0.0 797.9 jit_solution(10668589192870983978)
XLA Ops:
  9.8 2.4 collective-permute-start
  18.0 9.5 %fusion.103 = (f32[4,32]{1,0:T(4,128)S(1)}, f32[1,4,32,1536]{3,2,1,0:T(8,128)S(1)}) fusion(f32[1536]{0:T(1024)S(1)} %get-tuple-element.106, f32[1536]{0:T(1024)S(1)} %get-tuple-element.107, f32[1536]{0:T(1024)S(1)} %get-tuple-element.60, f32[1536]{0:T(1024)S(1)} %get-tuple-element.61, f32[1,10,32,1536]{3,2,1,0:T(8,128)S(1)} %maximum_convert_fusion, ...), kind=kLoop, calls=%fused_computation.314 | loop fusion | flops 19267456 | bytes 8641024 | tf_op jit(solution)/shard_map/reduce_sum | solution.py:55
  30.1 8.6 %all_gather.12 = bf16[256,1536]{1,0:T(8,128)(2,1)} all-gather(bf16[128,1536]{1,0:T(8,128)(2,1)S(1)} %multiply_convert_fusion.1), channel_id=1, replica_groups=mesh['dp'=4,'fsdp'=2,'rows'=4] {'fsdp'}, dimensions={0}, use_global_device_ids=true | all-gather | bytes 1179648 | tf_op jit(solution)/shard_map/all_gather | solution.py:61
  38.7 55.8 %all-gather.3.cloned.1.call-done = bf16[1536,3072]{1,0:T(8,128)(2,1)} async-done(((bf16[96,3072]{1,0:T(8,128)(2,1)}), bf16[1536,3072]{1,0:T(8,128)(2,1)}) %all-gather.3.cloned.1.call-update) | async-done | bytes 9437200 | tf_op jit(solution)/shard_map/all_gather | solution.py:62
  94.5 8.2 %fusion.106 = f32[256,3072]{1,0:T(8,128)} fusion(bf16[256,1536]{1,0:T(8,128)(2,1)} %all_gather.12, bf16[1536,3072]{1,0:T(8,128)(2,1)} %all-gather.3.cloned.1.call-done), kind=kOutput, calls=%fused_computation.317 | convolution fusion | flops 2415919104 | bytes 13369344 | tf_op jit(solution)/shard_map/dot_general | solution.py:64
  102.7 73.7 %all-gather.5.cloned.1.call-done = bf16[3072,1536]{0,1:T(8,128)(2,1)} async-done(((bf16[3072,96]{0,1:T(8,128)(2,1)}), bf16[3072,1536]{0,1:T(8,128)(2,1)}) %all-gather.5.cloned.1.call-update) | async-done | bytes 9437200 | tf_op jit(solution)/shard_map/all_gather | solution.py:63
  176.4 8.2 %convolution_convert_fusion = bf16[256,1536]{1,0:T(8,128)(2,1)} fusion(bf16[3072,1536]{0,1:T(8,128)(2,1)} %all-gather.5.cloned.1.call-done, f32[256,3072]{1,0:T(8,128)} %fusion.106), kind=kOutput, calls=%fused_computation.93 | convolution fusion | flops 2420244480 | bytes 13369344 | tf_op jit(solution)/shard_map/dot_general | solution.py:66
  184.6 15.7 %reduce-scatter.5.cloned.1.call-done = bf16[128,1536]{1,0:T(8,128)(2,1)} async-done(((bf16[256,1536]{1,0:T(8,128)(2,1)}), bf16[128,1536]{1,0:T(8,128)(2,1)}) %reduce-scatter.5.cloned.1.call-update) | async-done | bytes 393232 | tf_op jit(solution)/shard_map/reduce_scatter | solution.py:67
  200.3 2.7 fusion.7
  203.0 11.8 %all_gather.15 = bf16[256,1536]{1,0:T(8,128)(2,1)S(1)} all-gather(bf16[128,1536]{1,0:T(8,128)(2,1)S(1)} %get-tuple-element.114), channel_id=1, replica_groups=mesh['dp'=4,'fsdp'=2,'rows'=4] {'fsdp'}, dimensions={0}, use_global_device_ids=true | all-gather | bytes 1179648 | tf_op jit(solution)/shard_map/all_gather | solution.py:75
  215.7 5.5 fusion
  222.5 3.8 fusion.107
  226.4 26.2 %reduce-scatter.7.cloned.1.call-done = f32[128,1536]{1,0:T(8,128)} async-done(((f32[256,1536]{1,0:T(8,128)}), f32[128,1536]{1,0:T(8,128)}) %reduce-scatter.7.cloned.1.call-update) | async-done | bytes 786448 | tf_op jit(solution)/shard_map/reduce_scatter | solution.py:87
  252.6 2.0 multiply_reduce_fusion
  254.6 3.6 multiply_reduce_fusion.2
  259.4 2.0 multiply_reduce_fusion.1
  263.5 11.1 %fusion.102 = f32[3072,1536]{0,1:T(8,128)} fusion(bf16[256,1536]{1,0:T(8,128)(2,1)S(1)} %copy-done.3, f32[256,3072]{1,0:T(8,128)} %fusion.106), kind=kOutput, calls=%fused_computation.313 | convolution fusion | flops 2419851264 | bytes 22806528 | tf_op jit(solution)/shard_map/dot_general | solution.py:76
  276.2 7.9 fusion.108
  284.7 1.9 collective-permute-start.2
  287.9 42.3 %all-reduce.2 = (f32[1536]{0:T(1024)}, f32[1536]{0:T(1024)}) all-reduce(f32[1536]{0:T(1024)} %get-tuple-element.56, f32[1536]{0:T(1024)} %get-tuple-element.113), channel_id=1, replica_groups=mesh['dp'=4,'fsdp'=2,'rows'=4] {'dp','fsdp','rows'}, use_global_device_ids=true, to_apply=%region_59.60 | all-reduce | flops 3072 | bytes 24576 | tf_op jit(solution)/shard_map/psum | solution.py:115
  330.7 7.5 fusion.95
  338.3 51.2 %all-reduce.5.cloned.1.call-done = f32[7,7,1536]{2,1,0:T(8,128)} async-done(((f32[7,7,1536]{2,1,0:T(8,128)}), f32[7,7,1536]{2,1,0:T(8,128)}) %all-reduce.5.cloned.1.call-update) | async-done | bytes 301072 | tf_op jit(solution)/shard_map/psum | solution.py:115
  389.4 200.8 %reduce-scatter.11.cloned.1.call-done = f32[3072,96]{0,1:T(8,128)} async-done(((f32[3072,1536]{0,1:T(8,128)}), f32[3072,96]{0,1:T(8,128)}) %reduce-scatter.11.cloned.1.call-update) | async-done | bytes 1179664 | tf_op jit(solution)/shard_map/reduce_scatter | solution.py:38
  590.2 199.1 %reduce-scatter.9.cloned.1.call-done = f32[96,3072]{1,0:T(8,128)} async-done(((f32[1536,3072]{1,0:T(8,128)}), f32[96,3072]{1,0:T(8,128)}) %reduce-scatter.9.cloned.1.call-update) | async-done | bytes 1179664 | tf_op jit(solution)/shard_map/reduce_scatter | solution.py:88
  (278 shorter events, 20.6 us)
Async XLA Ops:
  7.2 87.3 %all-gather.3.cloned.1.call-start = ((), (), s32[]{:S(2)}) async-start(), calls=%async_computation.4 | async-start | bytes 10027008 | tf_op jit(solution)/shard_map/all_gather | solution.py:62
  7.9 168.5 %all-gather.5.cloned.1.call-start = ((), (), s32[]{:S(2)}) async-start(), calls=%async_computation.5 | async-start | bytes 10027008 | tf_op jit(solution)/shard_map/all_gather | solution.py:63
  8.7 191.6 %reduce-scatter.5.cloned.1.call-start = ((), (), s32[]{:S(2)}) async-start(), calls=%async_computation.6 | async-start | bytes 1179648 | tf_op jit(solution)/shard_map/reduce_scatter | solution.py:67
  9.8 6.6 collective-permute-start
  12.2 5.6 collective-permute-start.1
  102.7 97.6 %copy-start.5 = (bf16[1,4,32,1536]{3,2,1,0:T(8,128)(2,1)S(1)}, bf16[1,4,32,1536]{3,2,1,0:T(8,128)(2,1)}, u32[]{:S(2)}) copy-start(bf16[1,4,32,1536]{3,2,1,0:T(8,128)(2,1)} %param.13) | copy-start | bytes 1179652
  184.6 68.0 %reduce-scatter.7.cloned.1.call-start = ((), (), s32[]{:S(2)}) async-start(), calls=%async_computation.7 | async-start | bytes 2359296 | tf_op jit(solution)/shard_map/reduce_scatter | solution.py:87
  226.3 163.1 %all-reduce.5.cloned.1.call-start = ((), (), s32[]{:S(2)}) async-start(), calls=%async_computation.10 | async-start | bytes 688128 | tf_op jit(solution)/shard_map/psum | solution.py:115
  263.4 326.7 %reduce-scatter.11.cloned.1.call-start = ((), (), s32[]{:S(2)}) async-start(), calls=%async_computation.9 | async-start | bytes 20054016 | tf_op jit(solution)/shard_map/reduce_scatter | solution.py:38
  274.6 514.7 %reduce-scatter.9.cloned.1.call-start = ((), (), s32[]{:S(2)}) async-start(), calls=%async_computation.8 | async-start | bytes 20054016 | tf_op jit(solution)/shard_map/reduce_scatter | solution.py:88
  284.2 46.1 %copy-start.6 = (bf16[1,4,32,1536]{3,2,1,0:T(8,128)(2,1)S(1)}, bf16[1,4,32,1536]{3,2,1,0:T(8,128)(2,1)}, u32[]{:S(2)}) copy-start(bf16[1,4,32,1536]{3,2,1,0:T(8,128)(2,1)} %param.13) | copy-start | bytes 1179652
  284.2 46.1 %copy-start.12 = (f32[1536]{0:T(1024)S(1)}, f32[1536]{0:T(1024)}, u32[]{:S(2)}) copy-start(f32[1536]{0:T(1024)} %copy-done.11) | copy-start | bytes 18436
  284.2 46.1 %copy-start.14 = (f32[1536]{0:T(1024)S(1)}, f32[1536]{0:T(1024)}, u32[]{:S(2)}) copy-start(f32[1536]{0:T(1024)} %copy-done.13) | copy-start | bytes 18436
  284.2 46.1 %copy-start.16 = (f32[1536]{0:T(1024)S(1)}, f32[1536]{0:T(1024)}, u32[]{:S(2)}) copy-start(f32[1536]{0:T(1024)} %copy-done.15) | copy-start | bytes 18436
  284.2 46.1 %copy-start.18 = (f32[1536]{0:T(1024)S(1)}, f32[1536]{0:T(1024)}, u32[]{:S(2)}) copy-start(f32[1536]{0:T(1024)} %copy-done.17) | copy-start | bytes 18436
  284.3 46.1 %copy-start.20 = (f32[1536]{0:T(1024)S(1)}, f32[1536]{0:T(1024)}, u32[]{:S(2)}) copy-start(f32[1536]{0:T(1024)} %copy-done.19) | copy-start | bytes 18436
  284.3 46.1 %copy-start.22 = (f32[1536]{0:T(1024)S(1)}, f32[1536]{0:T(1024)}, u32[]{:S(2)}) copy-start(f32[1536]{0:T(1024)} %copy-done.21) | copy-start | bytes 18436
  284.3 46.1 %copy-start.24 = (f32[1536]{0:T(1024)S(1)}, f32[1536]{0:T(1024)}, u32[]{:S(2)}) copy-start(f32[1536]{0:T(1024)} %copy-done.23) | copy-start | bytes 18436
  284.3 46.1 %copy-start.26 = (f32[1536]{0:T(1024)S(1)}, f32[1536]{0:T(1024)}, u32[]{:S(2)}) copy-start(f32[1536]{0:T(1024)} %copy-done.25) | copy-start | bytes 18436
  284.3 46.1 %copy-start.28 = (f32[1536]{0:T(1024)S(1)}, f32[1536]{0:T(1024)}, u32[]{:S(2)}) copy-start(f32[1536]{0:T(1024)} %copy-done.27) | copy-start | bytes 18436
  284.3 46.1 %copy-start.30 = (f32[1536]{0:T(1024)S(1)}, f32[1536]{0:T(1024)}, u32[]{:S(2)}) copy-start(f32[1536]{0:T(1024)} %copy-done.29) | copy-start | bytes 18436
  284.3 46.1 %copy-start.32 = (f32[1536]{0:T(1024)S(1)}, f32[1536]{0:T(1024)}, u32[]{:S(2)}) copy-start(f32[1536]{0:T(1024)} %copy-done.31) | copy-start | bytes 18436
  284.7 45.5 %collective-permute-start.2 = (bf16[1,3,32,1536]{3,2,1,0:T(8,128)(2,1)S(1)}, bf16[1,3,32,1536]{3,2,1,0:T(8,128)(2,1)S(1)}, u32[]{:S(2)}, u32[]{:S(2)}) collective-permute-start(bf16[1,3,32,1536]{3,2,1,0:T(8,128)(2,1)S(1)} %get-tuple-element.116), channel_id=1, source_target_pairs={{0,1},{1,2},{2,3},{4,5},{5,6},{6,7},{8,9},{9,10},{10,11},{12,13},{... | collective-permute-start | bytes 884744 | tf_op jit(solution)/shard_map/ppermute | solution.py:22
  286.5 43.6 %collective-permute-start.3 = (bf16[1,3,32,1536]{3,2,1,0:T(8,128)(2,1)S(1)}, bf16[1,3,32,1536]{3,2,1,0:T(8,128)(2,1)S(1)}, u32[]{:S(2)}, u32[]{:S(2)}) collective-permute-start(bf16[1,3,32,1536]{3,2,1,0:T(8,128)(2,1)S(1)} %get-tuple-element.117), channel_id=1, source_target_pairs={{1,0},{2,1},{3,2},{5,4},{6,5},{7,6},{9,8},{10,9},{11,10},{13,12},{... | collective-permute-start | bytes 884744 | tf_op jit(solution)/shard_map/ppermute | solution.py:23
  (81 other events, 1911.3 us)
Sparse Core Ops, SparseCore 0:
  10.3 84.1 all-gather.2
  96.8 79.5 all-gather.4
  184.7 15.5 reduce-scatter.4
  226.4 26.0 reduce-scatter.6
  263.6 125.8 all-reduce.4
  394.5 195.6 reduce-scatter.10
  595.4 193.8 reduce-scatter.8
where the time goes:
time: 799 us; the launch traced here: 798 us
  waiting for transfers between devices  625 us (78%)
  blocking collectives  62.7 us (8%)
  matrix products  44.7 us (6%)
  other arithmetic  30 us (4%)
  between operations  16 us (2%)
  local copies, waits for them, and re-layouts  12.1 us (2%)
    reduce_scatter x1, waiting for transfers between devices, reduce_down(): lax.psum_scatter(down_part, ('dp', 'rows'), scatter_dimension=1, tiled=True)  201 us
    reduce_scatter x1, waiting for transfers between devices, body(): lax.psum_scatter(up_part, ('dp', 'rows'), scatter_dimension=0, tiled=True)  199 us
    all_gather x1, waiting for transfers between devices, body(): down_full = lax.all_gather(w_down, ('dp', 'rows'), axis=1, tiled=True)  73.7 us
    all_gather x1, waiting for transfers between devices, body(): up_full = lax.all_gather(w_up, ('dp', 'rows'), axis=0, tiled=True)  55.8 us
    psum x1, waiting for transfers between devices, body(): lax.psum((kernel_part, gain_part, scale_part), ('dp', 'fsdp', 'rows'))  51.2 us
    psum x1, blocking collectives, body(): lax.psum((kernel_part, gain_part, scale_part), ('dp', 'fsdp', 'rows'))  42.3 us
    reduce_scatter x1, waiting for transfers between devices, body(): lax.psum_scatter(norm_terms, 'fsdp', scatter_dimension=0, tiled=True)  26.2 us
  transfers between devices with their start and end apart: 11, of which 8 were waited for; matrix products, arithmetic and copies ran while one was open for 6% of the time, Pallas kernels for 0%

commit v1 on v0

--- a/solution.py
+++ b/solution.py
@@ -113,7 +113,7 @@
     kernel_part = jnp.stack(kernel_rows).reshape(KS, KS, width)
     grad_x = (d_out.astype(jnp.float32) + back_conv).astype(jnp.bfloat16)
     grad_kernel, grad_gain, grad_scale = lax.psum(
-        (kernel_part, gain_part, scale_part), ("dp", "fsdp", "rows")
+        lax.psum((kernel_part, gain_part, scale_part), ("fsdp", "rows")), "dp"
     )
     return (result, grad_x, grad_up, grad_down, grad_kernel, grad_gain, grad_scale)
 

time: 799 us -> 763 us (0.955)
  waiting for transfers between devices: 625 us -> 586 us
    reduce_scatter x1, waiting for transfers between devices: 201 us -> 161 us  [reduce_down(): lax.psum_scatter(down_part, ('dp', 'rows'), scatter_dimension=1, tiled=True)]
    psum x1 -> x2, blocking collectives: 42.3 us -> 44.7 us  [the longest x1 25.8 us: body(): lax.psum((kernel_part, gain_part, scale_part), ('fsdp', 'rows'))]
    psum x1 -> x2, waiting for transfers between devices: 51.2 us -> 52.7 us  [the longest x1 52.7 us: body(): lax.psum((kernel_part, gain_part, scale_part), ('fsdp', 'rows'))]
  transfers between devices with their start and end apart: 11 -> 12, of which waited for: 8 -> 8; matrix products, arithmetic and copies ran while one was open for 6% -> 7% of each run, Pallas kernels for 0% -> 0%
where the time goes in v1:
time: 763 us; the launch traced here: 762 us
  waiting for transfers between devices  586 us (77%)
  blocking collectives  65.2 us (9%)
  matrix products  44.7 us (6%)
  other arithmetic  30 us (4%)
  between operations  16 us (2%)
  local copies, waits for them, and re-layouts  12.1 us (2%)
  starting transfers between devices  7.97 us (1%)
    reduce_scatter x1, waiting for transfers between devices, body(): lax.psum_scatter(up_part, ('dp', 'rows'), scatter_dimension=0, tiled=True)  199 us
    reduce_scatter x1, waiting for transfers between devices, reduce_down(): lax.psum_scatter(down_part, ('dp', 'rows'), scatter_dimension=1, tiled=True)  161 us
    all_gather x1, waiting for transfers between devices, body(): down_full = lax.all_gather(w_down, ('dp', 'rows'), axis=1, tiled=True)  73.7 us
    all_gather x1, waiting for transfers between devices, body(): up_full = lax.all_gather(w_up, ('dp', 'rows'), axis=0, tiled=True)  55.8 us
    psum x1, waiting for transfers between devices, body(): lax.psum((kernel_part, gain_part, scale_part), ('fsdp', 'rows'))  52.7 us
    reduce_scatter x1, waiting for transfers between devices, body(): lax.psum_scatter(norm_terms, 'fsdp', scatter_dimension=0, tiled=True)  26.2 us
    psum x1, blocking collectives, body(): lax.psum((kernel_part, gain_part, scale_part), ('fsdp', 'rows'))  25.8 us
    psum x1, blocking collectives, body(): lax.psum(lax.psum((kernel_part, gain_part, scale_part), ('fsdp', 'rows'))...  18.9 us
  transfers between devices with their start and end apart: 12, of which 8 were waited for; matrix products, arithmetic and copies ran while one was open for 7% of the time, Pallas kernels for 0%

profile of v1, /device:TPU:0, one launch (start us, length us, event | category | flops | bytes accessed | tf_op | source)
XLA Modules:
  0.0 762.3 jit_solution(614729988281357002)
XLA Ops:
  9.8 2.4 collective-permute-start
  18.0 9.5 %fusion.103 = (f32[4,32]{1,0:T(4,128)S(1)}, f32[1,4,32,1536]{3,2,1,0:T(8,128)S(1)}) fusion(f32[1536]{0:T(1024)S(1)} %get-tuple-element.106, f32[1536]{0:T(1024)S(1)} %get-tuple-element.107, f32[1536]{0:T(1024)S(1)} %get-tuple-element.60, f32[1536]{0:T(1024)S(1)} %get-tuple-element.61, f32[1,10,32,1536]{3,2,1,0:T(8,128)S(1)} %maximum_convert_fusion, ...), kind=kLoop, calls=%fused_computation.314 | loop fusion | flops 19267456 | bytes 8641024 | tf_op jit(solution)/shard_map/reduce_sum | solution.py:55
  30.1 8.6 %all_gather.12 = bf16[256,1536]{1,0:T(8,128)(2,1)} all-gather(bf16[128,1536]{1,0:T(8,128)(2,1)S(1)} %multiply_convert_fusion.1), channel_id=1, replica_groups=mesh['dp'=4,'fsdp'=2,'rows'=4] {'fsdp'}, dimensions={0}, use_global_device_ids=true | all-gather | bytes 1179648 | tf_op jit(solution)/shard_map/all_gather | solution.py:61
  38.7 55.8 %all-gather.3.cloned.1.call-done = bf16[1536,3072]{1,0:T(8,128)(2,1)} async-done(((bf16[96,3072]{1,0:T(8,128)(2,1)}), bf16[1536,3072]{1,0:T(8,128)(2,1)}) %all-gather.3.cloned.1.call-update) | async-done | bytes 9437200 | tf_op jit(solution)/shard_map/all_gather | solution.py:62
  94.5 8.2 %fusion.106 = f32[256,3072]{1,0:T(8,128)} fusion(bf16[256,1536]{1,0:T(8,128)(2,1)} %all_gather.12, bf16[1536,3072]{1,0:T(8,128)(2,1)} %all-gather.3.cloned.1.call-done), kind=kOutput, calls=%fused_computation.317 | convolution fusion | flops 2415919104 | bytes 13369344 | tf_op jit(solution)/shard_map/dot_general | solution.py:64
  102.7 73.7 %all-gather.5.cloned.1.call-done = bf16[3072,1536]{0,1:T(8,128)(2,1)} async-done(((bf16[3072,96]{0,1:T(8,128)(2,1)}), bf16[3072,1536]{0,1:T(8,128)(2,1)}) %all-gather.5.cloned.1.call-update) | async-done | bytes 9437200 | tf_op jit(solution)/shard_map/all_gather | solution.py:63
  176.4 8.2 %convolution_convert_fusion = bf16[256,1536]{1,0:T(8,128)(2,1)} fusion(bf16[3072,1536]{0,1:T(8,128)(2,1)} %all-gather.5.cloned.1.call-done, f32[256,3072]{1,0:T(8,128)} %fusion.106), kind=kOutput, calls=%fused_computation.93 | convolution fusion | flops 2420244480 | bytes 13369344 | tf_op jit(solution)/shard_map/dot_general | solution.py:66
  184.6 15.7 %reduce-scatter.5.cloned.1.call-done = bf16[128,1536]{1,0:T(8,128)(2,1)} async-done(((bf16[256,1536]{1,0:T(8,128)(2,1)}), bf16[128,1536]{1,0:T(8,128)(2,1)}) %reduce-scatter.5.cloned.1.call-update) | async-done | bytes 393232 | tf_op jit(solution)/shard_map/reduce_scatter | solution.py:67
  200.3 2.7 fusion.7
  203.0 11.8 %all_gather.15 = bf16[256,1536]{1,0:T(8,128)(2,1)S(1)} all-gather(bf16[128,1536]{1,0:T(8,128)(2,1)S(1)} %get-tuple-element.116), channel_id=1, replica_groups=mesh['dp'=4,'fsdp'=2,'rows'=4] {'fsdp'}, dimensions={0}, use_global_device_ids=true | all-gather | bytes 1179648 | tf_op jit(solution)/shard_map/all_gather | solution.py:75
  215.7 5.5 fusion
  222.5 3.8 fusion.107
  226.4 26.2 %reduce-scatter.7.cloned.1.call-done = f32[128,1536]{1,0:T(8,128)} async-done(((f32[256,1536]{1,0:T(8,128)}), f32[128,1536]{1,0:T(8,128)}) %reduce-scatter.7.cloned.1.call-update) | async-done | bytes 786448 | tf_op jit(solution)/shard_map/reduce_scatter | solution.py:87
  254.6 3.6 multiply_reduce_fusion.2
  259.4 2.0 multiply_reduce_fusion.1
  263.5 52.7 %all-reduce.7.cloned.1.call-done = f32[7,7,1536]{2,1,0:T(8,128)} async-done(((f32[7,7,1536]{2,1,0:T(8,128)}), f32[7,7,1536]{2,1,0:T(8,128)}) %all-reduce.7.cloned.1.call-update) | async-done | bytes 301072 | tf_op jit(solution)/shard_map/psum | solution.py:116
  316.3 11.1 %fusion.102 = f32[3072,1536]{0,1:T(8,128)} fusion(bf16[256,1536]{1,0:T(8,128)(2,1)S(1)} %copy-done.3, f32[256,3072]{1,0:T(8,128)} %fusion.106), kind=kOutput, calls=%fused_computation.313 | convolution fusion | flops 2419851264 | bytes 22806528 | tf_op jit(solution)/shard_map/dot_general | solution.py:76
  329.0 7.9 %fusion.108 = f32[1536,3072]{1,0:T(8,128)} fusion(bf16[256,1536]{1,0:T(8,128)(2,1)S(1)} %copy-done.1, bf16[256,3072]{1,0:T(8,128)(2,1)S(1)} %copy-done.8), kind=kOutput, calls=%fused_computation.319 | convolution fusion | flops 2415919104 | bytes 21233664 | tf_op jit(solution)/shard_map/dot_general | solution.py:81
  337.5 2.5 collective-permute-start.2
  341.3 25.8 %all-reduce.2 = (f32[1536]{0:T(1024)S(1)}, f32[1536]{0:T(1024)S(1)}) all-reduce(f32[1536]{0:T(1024)} %get-tuple-element.56, f32[1536]{0:T(1024)} %get-tuple-element.115), channel_id=1, replica_groups=mesh['dp'=4,'fsdp'=2,'rows'=4] {'fsdp','rows'}, use_global_device_ids=true, to_apply=%region_60.61 | all-reduce | flops 3072 | bytes 24576 | tf_op jit(solution)/shard_map/psum | solution.py:116
  367.1 18.9 %all-reduce.3 = (f32[1536]{0:T(1024)}, f32[1536]{0:T(1024)}) all-reduce(f32[1536]{0:T(1024)S(1)} %get-tuple-element.108, f32[1536]{0:T(1024)S(1)} %get-tuple-element.109), channel_id=1, replica_groups=mesh['dp'=4,'fsdp'=2,'rows'=4] {'dp'}, use_global_device_ids=true, to_apply=%region_61.62 | all-reduce | flops 3072 | bytes 24576 | tf_op jit(solution)/shard_map/psum | solution.py:115
  386.6 7.6 fusion.95
  394.2 160.8 %reduce-scatter.11.cloned.1.call-done = f32[3072,96]{0,1:T(8,128)} async-done(((f32[3072,1536]{0,1:T(8,128)}), f32[3072,96]{0,1:T(8,128)}) %reduce-scatter.11.cloned.1.call-update) | async-done | bytes 1179664 | tf_op jit(solution)/shard_map/reduce_scatter | solution.py:38
  555.0 198.8 %reduce-scatter.9.cloned.1.call-done = f32[96,3072]{1,0:T(8,128)} async-done(((f32[1536,3072]{1,0:T(8,128)}), f32[96,3072]{1,0:T(8,128)}) %reduce-scatter.9.cloned.1.call-update) | async-done | bytes 1179664 | tf_op jit(solution)/shard_map/reduce_scatter | solution.py:88
  (282 shorter events, 22.6 us)
Async XLA Ops:
  7.2 87.3 %all-gather.3.cloned.1.call-start = ((), (), s32[]{:S(2)}) async-start(), calls=%async_computation.4 | async-start | bytes 10027008 | tf_op jit(solution)/shard_map/all_gather | solution.py:62
  7.9 168.5 %all-gather.5.cloned.1.call-start = ((), (), s32[]{:S(2)}) async-start(), calls=%async_computation.5 | async-start | bytes 10027008 | tf_op jit(solution)/shard_map/all_gather | solution.py:63
  8.7 191.6 %reduce-scatter.5.cloned.1.call-start = ((), (), s32[]{:S(2)}) async-start(), calls=%async_computation.6 | async-start | bytes 1179648 | tf_op jit(solution)/shard_map/reduce_scatter | solution.py:67
  9.8 6.6 collective-permute-start
  12.2 5.6 collective-permute-start.1
  102.7 97.6 %copy-start.5 = (bf16[1,4,32,1536]{3,2,1,0:T(8,128)(2,1)S(1)}, bf16[1,4,32,1536]{3,2,1,0:T(8,128)(2,1)}, u32[]{:S(2)}) copy-start(bf16[1,4,32,1536]{3,2,1,0:T(8,128)(2,1)} %param.13) | copy-start | bytes 1179652
  184.6 68.0 %reduce-scatter.7.cloned.1.call-start = ((), (), s32[]{:S(2)}) async-start(), calls=%async_computation.7 | async-start | bytes 2359296 | tf_op jit(solution)/shard_map/reduce_scatter | solution.py:87
  226.3 89.9 %all-reduce.7.cloned.1.call-start = ((), (), s32[]{:S(2)}) async-start(), calls=%async_computation.10 | async-start | bytes 688128 | tf_op jit(solution)/shard_map/psum | solution.py:116
  259.4 56.9 %copy-start.3 = (bf16[256,1536]{1,0:T(8,128)(2,1)S(1)}, bf16[256,1536]{1,0:T(8,128)(2,1)}, u32[]{:S(2)}) copy-start(bf16[256,1536]{1,0:T(8,128)(2,1)} %copy-done.2) | copy-start | bytes 2359300
  263.4 130.7 %all-reduce.9.cloned.1.call-start = ((), (), s32[]{:S(2)}) async-start(), calls=%async_computation.11 | async-start | bytes 688128 | tf_op jit(solution)/shard_map/psum | solution.py:115
  316.3 238.7 %reduce-scatter.11.cloned.1.call-start = ((), (), s32[]{:S(2)}) async-start(), calls=%async_computation.9 | async-start | bytes 20054016 | tf_op jit(solution)/shard_map/reduce_scatter | solution.py:38
  327.4 426.3 %reduce-scatter.9.cloned.1.call-start = ((), (), s32[]{:S(2)}) async-start(), calls=%async_computation.8 | async-start | bytes 20054016 | tf_op jit(solution)/shard_map/reduce_scatter | solution.py:88
  337.0 49.2 %copy-start.6 = (bf16[1,4,32,1536]{3,2,1,0:T(8,128)(2,1)S(1)}, bf16[1,4,32,1536]{3,2,1,0:T(8,128)(2,1)}, u32[]{:S(2)}) copy-start(bf16[1,4,32,1536]{3,2,1,0:T(8,128)(2,1)} %param.13) | copy-start | bytes 1179652
  337.0 49.2 %copy-start.12 = (f32[1536]{0:T(1024)S(1)}, f32[1536]{0:T(1024)}, u32[]{:S(2)}) copy-start(f32[1536]{0:T(1024)} %copy-done.11) | copy-start | bytes 18436
  337.0 49.2 %copy-start.14 = (f32[1536]{0:T(1024)S(1)}, f32[1536]{0:T(1024)}, u32[]{:S(2)}) copy-start(f32[1536]{0:T(1024)} %copy-done.13) | copy-start | bytes 18436
  337.0 49.2 %copy-start.16 = (f32[1536]{0:T(1024)S(1)}, f32[1536]{0:T(1024)}, u32[]{:S(2)}) copy-start(f32[1536]{0:T(1024)} %copy-done.15) | copy-start | bytes 18436
  337.1 49.2 %copy-start.18 = (f32[1536]{0:T(1024)S(1)}, f32[1536]{0:T(1024)}, u32[]{:S(2)}) copy-start(f32[1536]{0:T(1024)} %copy-done.17) | copy-start | bytes 18436
  337.1 49.2 %copy-start.20 = (f32[1536]{0:T(1024)S(1)}, f32[1536]{0:T(1024)}, u32[]{:S(2)}) copy-start(f32[1536]{0:T(1024)} %copy-done.19) | copy-start | bytes 18436
  337.1 49.2 %copy-start.22 = (f32[1536]{0:T(1024)S(1)}, f32[1536]{0:T(1024)}, u32[]{:S(2)}) copy-start(f32[1536]{0:T(1024)} %copy-done.21) | copy-start | bytes 18436
  337.1 49.2 %copy-start.24 = (f32[1536]{0:T(1024)S(1)}, f32[1536]{0:T(1024)}, u32[]{:S(2)}) copy-start(f32[1536]{0:T(1024)} %copy-done.23) | copy-start | bytes 18436
  337.1 49.2 %copy-start.26 = (f32[1536]{0:T(1024)S(1)}, f32[1536]{0:T(1024)}, u32[]{:S(2)}) copy-start(f32[1536]{0:T(1024)} %copy-done.25) | copy-start | bytes 18436
  337.1 49.2 %copy-start.28 = (f32[1536]{0:T(1024)S(1)}, f32[1536]{0:T(1024)}, u32[]{:S(2)}) copy-start(f32[1536]{0:T(1024)} %copy-done.27) | copy-start | bytes 18436
  337.5 48.6 %collective-permute-start.2 = (bf16[1,3,32,1536]{3,2,1,0:T(8,128)(2,1)S(1)}, bf16[1,3,32,1536]{3,2,1,0:T(8,128)(2,1)S(1)}, u32[]{:S(2)}, u32[]{:S(2)}) collective-permute-start(bf16[1,3,32,1536]{3,2,1,0:T(8,128)(2,1)S(1)} %get-tuple-element.118), channel_id=1, source_target_pairs={{0,1},{1,2},{2,3},{4,5},{5,6},{6,7},{8,9},{9,10},{10,11},{12,13},{... | collective-permute-start | bytes 884744 | tf_op jit(solution)/shard_map/ppermute | solution.py:22
  339.9 46.1 %collective-permute-start.3 = (bf16[1,3,32,1536]{3,2,1,0:T(8,128)(2,1)S(1)}, bf16[1,3,32,1536]{3,2,1,0:T(8,128)(2,1)S(1)}, u32[]{:S(2)}, u32[]{:S(2)}) collective-permute-start(bf16[1,3,32,1536]{3,2,1,0:T(8,128)(2,1)S(1)} %get-tuple-element.119), channel_id=1, source_target_pairs={{1,0},{2,1},{3,2},{5,4},{6,5},{7,6},{9,8},{10,9},{11,10},{13,12},{... | collective-permute-start | bytes 884744 | tf_op jit(solution)/shard_map/ppermute | solution.py:23
  (82 other events, 2090.4 us)
Sparse Core Ops, SparseCore 0:
  10.3 84.1 all-gather.2
  96.8 79.5 all-gather.4
  184.7 15.5 reduce-scatter.4
  226.4 26.0 reduce-scatter.6
  263.6 52.6 all-reduce.6
  318.4 37.1 all-reduce.8
  360.3 194.6 reduce-scatter.10
  559.7 194.0 reduce-scatter.8
